TPU v7x, 256 devices: a whole 4x4x8 slice. The times are simulated.
256 devices in a mesh: section: 16 (over y_lo, x, core), expert: 16 (over z, y_hi).
Axes of the slice: x: 4, y: 4 (y_hi: 2, y_lo: 2; y = y_hi * 2 + y_lo), z: 8, core: 2. Of those that a mesh axis runs over, the one named last changes fastest.
Arguments:
- activations: bfloat16 [16384, 8192], P('section', 'expert'), may hold values from -12 to 12
- modality: int32 [16384], P('section'), may hold values from 0 to 1
- selected: int32 [16, 256], P('section'), may hold values from 0 to 1023, as said below
- routes: int32 [4096, 1], P('section'), may hold values from 0 to 15, as said below
- norm_gain: float32 [2, 8192], P(None, 'expert'), may hold values from 0.1 to 1.9
- router: float32 [8192], P('expert'), may hold values from -0.0625 to 0.0625
- gate_w: bfloat16 [16, 3072, 8192], P('expert', 'section'), may hold values from -0.0625 to 0.0625
- up_w: bfloat16 [16, 3072, 8192], P('expert', 'section'), may hold values from -0.0625 to 0.0625
- down_w: bfloat16 [16, 3072, 8192], P('expert', 'section'), may hold values from -0.21875 to 0.21875
Outputs:
- block_out: bfloat16 [16384, 8192], P('section', 'expert')
Inputs may be any that keep to these rules, and one draw needn't show every extreme that they name: Each row of selected lists 256 different positions in rising order, the first and the last position among them. `routes`: among the 256 rows of one section group no expert is named more than 24 times, and some expert exactly 24 times; the entry for selected[s, j] is below 8 if that token's modality is 0, and 8 or more if it is 1.
All inputs are finite; a program needn't handle non-finite values.
Results may differ from a plain program's by a relative error of at most 0.0075.
Values may be sent and summed in bfloat16 or wider, within the bound.
No kernel may reach another device: no remote copies, remote signals or barrier semaphores. Data moves between devices by JAX's collectives and lax.ppermute only.
A program may use at most 128 MiB of HBM per device.

v0:
```python
import jax
import jax.numpy as jnp
from jax import lax
from jax.sharding import PartitionSpec as P

D = 8192
EPS = 1e-05


def passed_along(block, axis, distance):
    devices = range(lax.axis_size(axis))
    route = [((i - distance) % len(devices), i) for i in devices]
    return lax.ppermute(block, axis, route)


def feature_product(block, weight):
    return lax.dot_general(
        block, weight, (((1,), (1,)), ((), ())), preferred_element_type=jnp.float32
    )


def body(activations, modality, selected, routes, norm_gain, router, gate_w, up_w, down_w):
    arrived = passed_along(activations, "section", 1)
    picks = selected[0]
    picked = arrived[picks].astype(jnp.float32)
    kinds = modality[picks]
    gains = jnp.where(kinds[:, None] == 1, norm_gain[1][None, :], norm_gain[0][None, :])
    squares, router_terms = lax.psum(
        (jnp.sum(picked * picked, axis=1), jnp.sum(picked * gains * router[None, :], axis=1)),
        "expert",
    )
    scale = lax.rsqrt(squares / D + EPS)
    normed = (picked * scale[:, None] * gains).astype(jnp.bfloat16)
    score = jax.nn.sigmoid(scale * router_terms)
    sel_count = picks.shape[0]
    expert_count = lax.axis_size("expert") * gate_w.shape[0]
    capacity = max(2, 3 * sel_count // (2 * expert_count))
    experts = routes[:, 0]
    onehot = (experts[:, None] == jnp.arange(expert_count, dtype=jnp.int32)[None, :]).astype(
        jnp.int32
    )
    ranks = jnp.cumsum(onehot, axis=0) - 1
    slot = jnp.sum(ranks * onehot, axis=1)
    target = experts * capacity + slot
    placing = (
        target[None, :] == jnp.arange(expert_count * capacity, dtype=jnp.int32)[:, None]
    ).astype(jnp.bfloat16)
    feature_width = normed.shape[1]
    buffer = jnp.dot(placing, normed, preferred_element_type=jnp.float32).astype(jnp.bfloat16)
    buffer = buffer.reshape(expert_count, capacity, feature_width)
    arrived_rows = lax.all_to_all(buffer, "expert", split_axis=0, concat_axis=2, tiled=True)
    block = lax.all_gather(arrived_rows, "section", axis=1, tiled=True)[0]
    gate = feature_product(block, gate_w[0])
    upper = feature_product(block, up_w[0])
    hidden = (jax.nn.silu(gate) * upper).astype(jnp.bfloat16)[None][0]
    part = jnp.dot(hidden, down_w[0], preferred_element_type=jnp.float32)
    summed = lax.psum_scatter(
        lax.optimization_barrier(part.astype(jnp.bfloat16))
        .astype(jnp.float32)
        .astype(jnp.bfloat16),
        "section",
        scatter_dimension=0,
        tiled=True,
    )
    expert_out = summed[None]
    gathered_back = lax.all_to_all(expert_out, "expert", split_axis=2, concat_axis=0, tiled=True)
    flat_back = gathered_back.reshape(expert_count * capacity, feature_width)
    rows_out = jnp.dot(placing.T, flat_back, preferred_element_type=jnp.float32)
    result = arrived.astype(jnp.float32).at[picks].add(score[:, None] * rows_out)
    return result.astype(jnp.bfloat16)


def solution(mesh):
    placed = (
        P("section", "expert"),
        P("section"),
        P("section", None),
        P("section", None),
        P(None, "expert"),
        P("expert"),
        P("expert", "section", None),
        P("expert", "section", None),
        P("expert", "section", None),
    )
    return jax.shard_map(
        body, mesh=mesh, in_specs=placed, out_specs=P("section", "expert"), check_vma=False
    )
```

profile of v0, /device:TPU:7, one launch (start us, length us, event | category | flops | bytes accessed | tf_op | source)
XLA Modules:
  0.0 331.5 jit_solution(17080276669654069664)
XLA Ops:
  6.5 0.0 copy-start
  6.5 0.0 copy-start.1
  6.5 0.0 all-gather.2.cloned.1.call-start
  6.5 1.8 collective-permute-start
  8.3 0.7 fusion.30
  9.0 0.6 reduce-window.6
  9.6 0.2 slice_reduce_fusion
  9.8 0.7 compare_select_fusion
  10.5 1.9 gather_fusion.1
  12.4 0.8 fusion.29
  13.2 0.7 multiply_add_fusion
  13.9 0.8 fusion.31
  14.6 5.7 %collective-permute-done = bf16[1024,512]{1,0:T(8,128)(2,1)} collective-permute-done((bf16[1024,512]{1,0:T(8,128)(2,1)}, bf16[1024,512]{1,0:T(8,128)(2,1)}, u32[]{:S(2)}, u32[]{:S(2)}) %collective-permute-start) | collective-permute-done | bytes 1048608 | tf_op jit(solution)/shard_map/ppermute | solution.py:13
  20.4 2.6 gather_fusion
  22.9 0.0 copy-done.1
  23.0 0.3 fusion.20
  23.2 37.6 %all-reduce = (f32[256]{0:T(256)S(1)}, f32[256]{0:T(256)S(1)}) all-reduce(f32[256]{0:T(256)S(1)} %get-tuple-element.6, f32[256]{0:T(256)S(1)} %get-tuple-element.5), channel_id=1, replica_groups=mesh['section'=16,'expert'=16] {'expert'}, use_global_device_ids=true, to_apply=%region_1.2 | all-reduce | flops 512 | bytes 4096 | tf_op jit(solution)/shard_map/psum | solution.py:28
  60.8 0.4 convolution_convert_fusion.1
  61.2 15.3 %all_to_all.33 = bf16[16,24,512]{2,1,0:T(8,128)(2,1)S(1)} all-to-all(bf16[16,24,512]{2,1,0:T(8,128)(2,1)S(1)} %bitcast.72), channel_id=1, replica_groups=mesh['section'=16,'expert'=16] {'expert'}, dimensions={0} | all-to-all | bytes 786432 | tf_op jit(solution)/shard_map/all_to_all | solution.py:51
  76.6 0.8 copy.22
  77.3 0.0 all-gather.2.cloned.1.call-update
  77.4 0.0 reduce-scatter.2.cloned.1.call-start
  77.4 49.9 %all-gather.2.cloned.1.call-done = bf16[1,384,8192]{2,1,0:T(8,128)(2,1)} async-done(((bf16[1,24,8192]{2,1,0:T(8,128)(2,1)}), bf16[1,384,8192]{2,1,0:T(8,128)(2,1)}) %all-gather.2.cloned.1.call-update) | async-done | bytes 6291472 | tf_op jit(solution)/shard_map/all_gather | solution.py:52
  127.3 0.0 copy-start.2
  127.3 0.0 copy-start.3
  127.3 6.1 %fusion.2 = f32[384,192]{0,1:T(8,128)S(1)} fusion(bf16[1,384,8192]{2,1,0:T(8,128)(2,1)} %all-gather.2.cloned.1.call-done, bf16[1,192,8192]{2,1,0:T(8,128)(2,1)} %param.15), kind=kOutput, calls=%fused_computation.6 | convolution fusion | flops 1207959552 | bytes 9732096 | tf_op jit(solution)/shard_map/dot_general | solution.py:17
  133.4 0.0 copy-done.2
  133.4 0.3 copy-done.3
  133.7 2.2 fusion.12
  136.0 0.0 copy-done
  136.0 4.5 %convolution_convert_fusion = bf16[384,8192]{1,0:T(8,128)(2,1)} fusion(bf16[384,192]{0,1:T(8,128)(2,1)S(1)} %fusion.12, bf16[1,192,8192]{2,1,0:T(8,128)(2,1)S(1)} %copy-done), kind=kOutput, calls=%fused_computation.3 | convolution fusion | flops 1211105280 | bytes 9584640 | tf_op jit(solution)/shard_map/dot_general | solution.py:56
  140.5 0.0 reduce-scatter.2.cloned.1.call-update
  140.5 72.4 %reduce-scatter.2.cloned.1.call-done = bf16[24,8192]{1,0:T(8,128)(2,1)} async-done(((bf16[384,8192]{1,0:T(8,128)(2,1)}), bf16[24,8192]{1,0:T(8,128)(2,1)}) %reduce-scatter.2.cloned.1.call-update) | async-done | bytes 393232 | tf_op jit(solution)/shard_map/reduce_scatter | solution.py:57
  212.9 8.4 %copy.18 = bf16[1,24,8192]{1,0,2:T(2,128)(2,1)} copy(bf16[1,24,8192]{2,1,0:T(8,128)(2,1)} %bitcast.71) | data formatting | bytes 786432 | tf_op jit(solution)/shard_map/broadcast_in_dim | solution.py:65
  221.3 0.5 broadcast.80
  221.8 46.5 %reduce.2 = bf16[8192,24]{1,0:T(8,128)(2,1)} reduce(bf16[8192,1,24]{2,1,0:T(2,128)(2,1)} %bitcast.64, bf16[]{:T(256)} %broadcast.80), dimensions={1}, to_apply=%bitcast.58.reduce_sub_computation | reduce | bytes 786434
  268.4 4.9 %reshape.96 = bf16[16,2,6144]{2,1,0:T(2,128)(2,1)} reshape(bf16[8192,24]{1,0:T(8,128)(2,1)} %reduce.2) | data formatting | bytes 786432
  273.3 8.9 %all-to-all-start.1 = ((bf16[16,2,6144]{2,1,0:T(2,128)(2,1)}), bf16[16,2,6144]{2,1,0:T(2,128)(2,1)S(1)}, u32[]{:S(2)}, u32[]{:S(2)}) async-start(bf16[16,2,6144]{2,1,0:T(2,128)(2,1)} %reshape.96), calls=%async_computation.2 | async-start | bytes 786432 | tf_op jit(solution)/shard_map/all_to_all | solution.py:66
  282.2 2.8 convert_element_type.29
  285.1 13.0 %all-to-all-done.1 = bf16[16,2,6144]{2,1,0:T(2,128)(2,1)S(1)} async-done(((bf16[16,2,6144]{2,1,0:T(2,128)(2,1)}), bf16[16,2,6144]{2,1,0:T(2,128)(2,1)S(1)}, u32[]{:S(2)}, u32[]{:S(2)}) %all-to-all-start.1) | async-done | bytes 393248 | tf_op jit(solution)/shard_map/all_to_all | solution.py:66
  298.1 8.9 %reshape.97 = bf16[8192,1,24]{2,1,0:T(2,128)(2,1)} reshape(bf16[16,2,6144]{2,1,0:T(2,128)(2,1)S(1)} %all-to-all-done.1) | data formatting | bytes 786432
  307.0 8.0 %copy.19 = bf16[1,24,8192]{2,1,0:T(8,128)(2,1)S(1)} copy(bf16[1,24,8192]{1,0,2:T(2,128)(2,1)} %bitcast.65) | data formatting | bytes 786432 | tf_op jit(solution)/shard_map/all_to_all | solution.py:66
  315.0 0.1 copy.23
  315.2 0.2 copy.20
  315.4 1.2 convolution_multiply_fusion
  316.6 5.4 %scatter_fusion = f32[1024,512]{1,0:T(8,128)} fusion(f32[1024,512]{1,0:T(8,128)} %convert_element_type.29, s32[256]{0:T(256)S(1)} %bitcast.74, f32[256,512]{1,0:T(8,128)} %convolution_multiply_fusion), kind=kCustom, calls=%fused_computation.2 | custom fusion | flops 131072 | bytes 1573888 | tf_op jit(solution)/shard_map/scatter-add | solution.py:69
  322.0 2.7 convert_element_type.36
  (6 shorter events, 0.1 us)
Async XLA Ops:
  6.5 129.4 %copy-start = (bf16[1,192,8192]{2,1,0:T(8,128)(2,1)S(1)}, bf16[1,192,8192]{2,1,0:T(8,128)(2,1)}, u32[]{:S(2)}) copy-start(bf16[1,192,8192]{2,1,0:T(8,128)(2,1)} %param.17) | copy-start | bytes 9437188
  6.5 16.4 %copy-start.1 = (f32[512]{0:T(512)S(1)}, f32[512]{0:T(512)}, u32[]{:S(2)}) copy-start(f32[512]{0:T(512)} %param.14) | copy-start | bytes 6148
  6.5 120.8 %all-gather.2.cloned.1.call-start = ((), (), s32[]{:S(2)}) async-start(), calls=%async_computation.3 | async-start | bytes 6684672 | tf_op jit(solution)/shard_map/all_gather | solution.py:52
  6.5 13.8 %collective-permute-start = (bf16[1024,512]{1,0:T(8,128)(2,1)}, bf16[1024,512]{1,0:T(8,128)(2,1)}, u32[]{:S(2)}, u32[]{:S(2)}) collective-permute-start(bf16[1024,512]{1,0:T(8,128)(2,1)} %param.9), channel_id=1, source_target_pairs={{240,0},{0,16},{16,32},{32,48},{48,64},{64,80},{80,96},{96,112},{1... | collective-permute-start | bytes 3145736 | tf_op jit(solution)/shard_map/ppermute | solution.py:13
  77.4 135.5 %reduce-scatter.2.cloned.1.call-start = ((), (), s32[]{:S(2)}) async-start(), calls=%async_computation.4 | async-start | bytes 6684672 | tf_op jit(solution)/shard_map/reduce_scatter | solution.py:57
  127.3 6.1 %copy-start.2 = (bf16[1,384,8192]{2,1,0:T(8,128)(2,1)S(1)}, bf16[1,384,8192]{2,1,0:T(8,128)(2,1)}, u32[]{:S(2)}) copy-start(bf16[1,384,8192]{2,1,0:T(8,128)(2,1)} %all-gather.2.cloned.1.call-done) | copy-start | bytes 18874372
  127.3 6.4 %copy-start.3 = (bf16[1,192,8192]{2,1,0:T(8,128)(2,1)S(1)}, bf16[1,192,8192]{2,1,0:T(8,128)(2,1)}, u32[]{:S(2)}) copy-start(bf16[1,192,8192]{2,1,0:T(8,128)(2,1)} %param.16) | copy-start | bytes 9437188
  273.3 24.8 %all-to-all-start.1 = ((bf16[16,2,6144]{2,1,0:T(2,128)(2,1)}), bf16[16,2,6144]{2,1,0:T(2,128)(2,1)S(1)}, u32[]{:S(2)}, u32[]{:S(2)}) async-start(bf16[16,2,6144]{2,1,0:T(2,128)(2,1)} %reshape.96), calls=%async_computation.2 | async-start | bytes 786432 | tf_op jit(solution)/shard_map/all_to_all | solution.py:66
Sparse Core Ops, SparseCore 0:
  77.5 49.7 all-gather.1
  140.6 72.2 reduce-scatter.1
where the time goes:
time: 333 us; the launch traced here: 332 us
  waiting for transfers between devices  141 us (42%)
  other arithmetic  61.3 us (18%)
  blocking collectives  52.9 us (16%)
  local copies, waits for them, and re-layouts  37.7 us (11%)
  matrix products  14.3 us (4%)
  between operations  13.5 us (4%)
  starting transfers between devices  10.7 us (3%)
    reduce_scatter x1, waiting for transfers between devices, body(): lax.psum_scatter(lax.optimization_barrier(part.astype(jnp.bfloat16)).asty...  72.4 us
    all_gather x1, waiting for transfers between devices, body(): block = lax.all_gather(arrived_rows, 'section', axis=1, tiled=True)[0]  49.9 us
    unnamed x1, other arithmetic  46.5 us
    psum x1, blocking collectives, body(): lax.psum((jnp.sum(picked * picked, axis=1), jnp.sum(picked * gains * rout...  37.6 us
    all_to_all x1, blocking collectives, body(): lax.all_to_all(buffer, 'expert', split_axis=0, concat_axis=2, tiled=True)  15.3 us
    unnamed x12, local copies, waits for them, and re-layouts  14.8 us
    all_to_all x1, waiting for transfers between devices, body(): lax.all_to_all(expert_out, 'expert', split_axis=2, concat_axis=0, tiled=T...  13 us
    all_to_all x1, starting transfers between devices, body(): lax.all_to_all(expert_out, 'expert', split_axis=2, concat_axis=0, tiled=T...  8.93 us
  transfers between devices with their start and end apart: 4, of which 4 were waited for; matrix products, arithmetic and copies ran while one was open for 3% of the time, Pallas kernels for 0%

commit v1 on v0

--- a/solution.py
+++ b/solution.py
@@ -63,7 +63,12 @@
         tiled=True,
     )
     expert_out = summed[None]
-    gathered_back = lax.all_to_all(expert_out, "expert", split_axis=2, concat_axis=0, tiled=True)
+    gathered_back = jnp.concatenate(
+        lax.all_to_all(
+            jnp.stack(jnp.split(expert_out, lax.axis_size("expert"), axis=2)), "expert", 0, 0
+        ),
+        axis=0,
+    )
     flat_back = gathered_back.reshape(expert_count * capacity, feature_width)
     rows_out = jnp.dot(placing.T, flat_back, preferred_element_type=jnp.float32)
     result = arrived.astype(jnp.float32).at[picks].add(score[:, None] * rows_out)

time: 333 us -> 277 us (0.83)
  other arithmetic: 61.3 us -> 14.8 us
  local copies, waits for them, and re-layouts: 37.7 us -> 28.1 us
    unnamed x1 -> x0, other arithmetic: 46.5 us -> none
    broadcast_in_dim x1 -> x0, local copies, waits for them, and re-layouts: 8.43 us -> none  [body(): expert_out = summed[None]]
    all_to_all x3 -> x0, local copies, waits for them, and re-layouts: 8.24 us -> none  [body(): lax.all_to_all(expert_out, 'expert', split_axis=2, concat_axis=0, tiled=T...]
    unnamed x12 -> x23, local copies, waits for them, and re-layouts: 14.8 us -> 20.5 us
where the time goes in v1:
time: 277 us; the launch traced here: 275 us
  waiting for transfers between devices  141 us (51%)
  blocking collectives  52.9 us (19%)
  local copies, waits for them, and re-layouts  28.1 us (10%)
  other arithmetic  14.8 us (5%)
  matrix products  14.3 us (5%)
  between operations  13.5 us (5%)
  starting transfers between devices  10.8 us (4%)
    reduce_scatter x1, waiting for transfers between devices, body(): lax.psum_scatter(lax.optimization_barrier(part.astype(jnp.bfloat16)).asty...  72.4 us
    all_gather x1, waiting for transfers between devices, body(): block = lax.all_gather(arrived_rows, 'section', axis=1, tiled=True)[0]  49.9 us
    psum x1, blocking collectives, body(): lax.psum((jnp.sum(picked * picked, axis=1), jnp.sum(picked * gains * rout...  37.6 us
    unnamed x23, local copies, waits for them, and re-layouts  20.5 us
    all_to_all x1, blocking collectives, body(): lax.all_to_all(buffer, 'expert', split_axis=0, concat_axis=2, tiled=True)  15.3 us
    all_to_all x1, waiting for transfers between devices, body(): lax.all_to_all(jnp.stack(jnp.split(expert_out, lax.axis_size('expert'), a...  13 us
    all_to_all x1, starting transfers between devices, body(): lax.all_to_all(jnp.stack(jnp.split(expert_out, lax.axis_size('expert'), a...  8.96 us
    dot_general x2, matrix products, feature_product(): lax.dot_general(block, weight, (((1,), (1,)), ((), ())), preferred_elemen...  8.28 us
  transfers between devices with their start and end apart: 4, of which 4 were waited for; matrix products, arithmetic and copies ran while one was open for 3% of the time, Pallas kernels for 0%

profile of v1, /device:TPU:7, one launch (start us, length us, event | category | flops | bytes accessed | tf_op | source)
XLA Modules:
  0.0 275.4 jit_solution(11247908684963835581)
XLA Ops:
  6.5 0.0 copy-start
  6.5 0.0 copy-start.1
  6.5 0.0 all-gather.2.cloned.1.call-start
  6.5 1.8 collective-permute-start
  8.3 0.7 fusion.30
  9.0 0.6 reduce-window.6
  9.6 0.2 slice_reduce_fusion
  9.8 0.7 compare_select_fusion
  10.5 1.9 gather_fusion.1
  12.4 0.8 fusion.29
  13.2 0.7 multiply_add_fusion
  13.9 0.8 fusion.31
  14.6 5.7 %collective-permute-done = bf16[1024,512]{1,0:T(8,128)(2,1)} collective-permute-done((bf16[1024,512]{1,0:T(8,128)(2,1)}, bf16[1024,512]{1,0:T(8,128)(2,1)}, u32[]{:S(2)}, u32[]{:S(2)}) %collective-permute-start) | collective-permute-done | bytes 1048608 | tf_op jit(solution)/shard_map/ppermute | solution.py:13
  20.4 2.6 gather_fusion
  22.9 0.0 copy-done.1
  23.0 0.3 fusion.20
  23.2 37.6 %all-reduce = (f32[256]{0:T(256)S(1)}, f32[256]{0:T(256)S(1)}) all-reduce(f32[256]{0:T(256)S(1)} %get-tuple-element.6, f32[256]{0:T(256)S(1)} %get-tuple-element.5), channel_id=1, replica_groups=mesh['section'=16,'expert'=16] {'expert'}, use_global_device_ids=true, to_apply=%region_1.2 | all-reduce | flops 512 | bytes 4096 | tf_op jit(solution)/shard_map/psum | solution.py:28
  60.8 0.4 convolution_convert_fusion.1
  61.2 15.3 %all_to_all.23 = bf16[16,24,512]{2,1,0:T(8,128)(2,1)S(1)} all-to-all(bf16[16,24,512]{2,1,0:T(8,128)(2,1)S(1)} %bitcast.137), channel_id=1, replica_groups=mesh['section'=16,'expert'=16] {'expert'}, dimensions={0} | all-to-all | bytes 786432 | tf_op jit(solution)/shard_map/all_to_all | solution.py:51
  76.6 0.8 copy.15
  77.3 0.0 all-gather.2.cloned.1.call-update
  77.4 0.0 reduce-scatter.2.cloned.1.call-start
  77.4 49.9 %all-gather.2.cloned.1.call-done = bf16[1,384,8192]{2,1,0:T(8,128)(2,1)} async-done(((bf16[1,24,8192]{2,1,0:T(8,128)(2,1)}), bf16[1,384,8192]{2,1,0:T(8,128)(2,1)}) %all-gather.2.cloned.1.call-update) | async-done | bytes 6291472 | tf_op jit(solution)/shard_map/all_gather | solution.py:52
  127.3 0.0 copy-start.2
  127.3 0.0 copy-start.3
  127.3 6.1 %fusion.2 = f32[384,192]{0,1:T(8,128)S(1)} fusion(bf16[1,384,8192]{2,1,0:T(8,128)(2,1)} %all-gather.2.cloned.1.call-done, bf16[1,192,8192]{2,1,0:T(8,128)(2,1)} %param.15), kind=kOutput, calls=%fused_computation.6 | convolution fusion | flops 1207959552 | bytes 9732096 | tf_op jit(solution)/shard_map/dot_general | solution.py:17
  133.4 0.0 copy-done.2
  133.4 0.3 copy-done.3
  133.7 2.2 fusion.12
  135.9 0.0 copy-done
  135.9 4.5 %convolution_convert_fusion = bf16[384,8192]{1,0:T(8,128)(2,1)} fusion(bf16[384,192]{0,1:T(8,128)(2,1)S(1)} %fusion.12, bf16[1,192,8192]{2,1,0:T(8,128)(2,1)S(1)} %copy-done), kind=kOutput, calls=%fused_computation.3 | convolution fusion | flops 1211105280 | bytes 9584640 | tf_op jit(solution)/shard_map/dot_general | solution.py:56
  140.4 0.0 reduce-scatter.2.cloned.1.call-update
  140.5 72.4 %reduce-scatter.2.cloned.1.call-done = bf16[24,8192]{1,0:T(8,128)(2,1)} async-done(((bf16[384,8192]{1,0:T(8,128)(2,1)}), bf16[24,8192]{1,0:T(8,128)(2,1)}) %reduce-scatter.2.cloned.1.call-update) | async-done | bytes 393232 | tf_op jit(solution)/shard_map/reduce_scatter | solution.py:57
  212.9 1.3 constant_dynamic-update-slice_fusion.15
  214.2 1.3 constant_dynamic-update-slice_fusion.14
  215.6 1.3 constant_dynamic-update-slice_fusion.13
  216.9 1.3 constant_dynamic-update-slice_fusion.12
  218.3 1.3 constant_dynamic-update-slice_fusion.11
  219.6 1.3 constant_dynamic-update-slice_fusion.10
  220.9 1.3 constant_dynamic-update-slice_fusion.9
  222.3 1.3 constant_dynamic-update-slice_fusion.8
  223.6 1.3 constant_dynamic-update-slice_fusion.7
  225.0 1.3 constant_dynamic-update-slice_fusion.6
  226.3 1.3 constant_dynamic-update-slice_fusion.5
  227.7 1.3 constant_dynamic-update-slice_fusion.4
  229.0 1.3 constant_dynamic-update-slice_fusion.3
  230.4 1.3 constant_dynamic-update-slice_fusion.2
  231.7 1.3 constant_dynamic-update-slice_fusion.1
  233.1 1.3 constant_dynamic-update-slice_fusion
  234.4 9.0 %all-to-all-start.1 = ((bf16[16,1,24,512]{3,2,1,0:T(8,128)(2,1)}), bf16[16,1,24,512]{3,2,1,0:T(8,128)(2,1)S(1)}, u32[]{:S(2)}, u32[]{:S(2)}) async-start(bf16[16,1,24,512]{3,2,1,0:T(8,128)(2,1)} %constant_dynamic-update-slice_fusion), calls=%async_computation.2 | async-start | bytes 786432 | tf_op jit(solution)/shard_map/all_to_all | solution.py:67
  243.4 2.9 %convert_element_type.29 = f32[1024,512]{1,0:T(8,128)} convert(bf16[1024,512]{1,0:T(8,128)(2,1)} %collective-permute-done) | non-fusion elementwise | flops 524288 | bytes 3145728 | tf_op jit(solution)/shard_map/convert_element_type | solution.py:74
  246.3 13.0 %all-to-all-done.1 = bf16[16,1,24,512]{3,2,1,0:T(8,128)(2,1)S(1)} async-done(((bf16[16,1,24,512]{3,2,1,0:T(8,128)(2,1)}), bf16[16,1,24,512]{3,2,1,0:T(8,128)(2,1)S(1)}, u32[]{:S(2)}, u32[]{:S(2)}) %all-to-all-start.1) | async-done | bytes 393248 | tf_op jit(solution)/shard_map/all_to_all | solution.py:67
  259.2 1.1 convolution_multiply_fusion
  260.4 5.5 %scatter_fusion = f32[1024,512]{1,0:T(8,128)} fusion(f32[1024,512]{1,0:T(8,128)} %convert_element_type.29, s32[256]{0:T(256)S(1)} %bitcast.139, f32[256,512]{1,0:T(8,128)} %convolution_multiply_fusion), kind=kCustom, calls=%fused_computation.2 | custom fusion | flops 131072 | bytes 1573888 | tf_op jit(solution)/shard_map/scatter-add | solution.py:74
  265.8 2.7 convert_element_type.36
  (5 shorter events, 0.1 us)
Async XLA Ops:
  6.5 129.4 %copy-start = (bf16[1,192,8192]{2,1,0:T(8,128)(2,1)S(1)}, bf16[1,192,8192]{2,1,0:T(8,128)(2,1)}, u32[]{:S(2)}) copy-start(bf16[1,192,8192]{2,1,0:T(8,128)(2,1)} %param.17) | copy-start | bytes 9437188
  6.5 16.4 %copy-start.1 = (f32[512]{0:T(512)S(1)}, f32[512]{0:T(512)}, u32[]{:S(2)}) copy-start(f32[512]{0:T(512)} %param.14) | copy-start | bytes 6148
  6.5 120.8 %all-gather.2.cloned.1.call-start = ((), (), s32[]{:S(2)}) async-start(), calls=%async_computation.3 | async-start | bytes 6684672 | tf_op jit(solution)/shard_map/all_gather | solution.py:52
  6.5 13.8 %collective-permute-start = (bf16[1024,512]{1,0:T(8,128)(2,1)}, bf16[1024,512]{1,0:T(8,128)(2,1)}, u32[]{:S(2)}, u32[]{:S(2)}) collective-permute-start(bf16[1024,512]{1,0:T(8,128)(2,1)} %param.9), channel_id=1, source_target_pairs={{240,0},{0,16},{16,32},{32,48},{48,64},{64,80},{80,96},{96,112},{1... | collective-permute-start | bytes 3145736 | tf_op jit(solution)/shard_map/ppermute | solution.py:13
  77.4 135.5 %reduce-scatter.2.cloned.1.call-start = ((), (), s32[]{:S(2)}) async-start(), calls=%async_computation.4 | async-start | bytes 6684672 | tf_op jit(solution)/shard_map/reduce_scatter | solution.py:57
  127.3 6.1 %copy-start.2 = (bf16[1,384,8192]{2,1,0:T(8,128)(2,1)S(1)}, bf16[1,384,8192]{2,1,0:T(8,128)(2,1)}, u32[]{:S(2)}) copy-start(bf16[1,384,8192]{2,1,0:T(8,128)(2,1)} %all-gather.2.cloned.1.call-done) | copy-start | bytes 18874372
  127.3 6.4 %copy-start.3 = (bf16[1,192,8192]{2,1,0:T(8,128)(2,1)S(1)}, bf16[1,192,8192]{2,1,0:T(8,128)(2,1)}, u32[]{:S(2)}) copy-start(bf16[1,192,8192]{2,1,0:T(8,128)(2,1)} %param.16) | copy-start | bytes 9437188
  234.4 24.8 %all-to-all-start.1 = ((bf16[16,1,24,512]{3,2,1,0:T(8,128)(2,1)}), bf16[16,1,24,512]{3,2,1,0:T(8,128)(2,1)S(1)}, u32[]{:S(2)}, u32[]{:S(2)}) async-start(bf16[16,1,24,512]{3,2,1,0:T(8,128)(2,1)} %constant_dynamic-update-slice_fusion), calls=%async_computation.2 | async-start | bytes 786432 | tf_op jit(solution)/shard_map/all_to_all | solution.py:67
Sparse Core Ops, SparseCore 0:
  77.5 49.7 all-gather.1
  140.6 72.2 reduce-scatter.1
